TPU v7x, 512 devices: a whole 4x4x16 slice. The times are simulated.
512 devices in a mesh: seq: 64 (over z_lo, x, core), dp: 8 (over y, z_hi).
Axes of the slice: x: 4, y: 4, z: 16 (z_hi: 2, z_lo: 8; z = z_hi * 8 + z_lo), core: 2. Of those that a mesh axis runs over, the one named last changes fastest.
Arguments:
- queries: bfloat16 [65536, 2048], P(('dp', 'seq')), parts along dimension 0, may hold values from -20 to 20
- keys: bfloat16 [65536, 2048], P(('dp', 'seq')), parts along dimension 0, may hold values from -20 to 20
- values: bfloat16 [65536, 2048], P(('dp', 'seq')), parts along dimension 0, may hold values from -48 to 48
- cotangent: bfloat16 [65536, 2048], P(('dp', 'seq')), parts along dimension 0, may hold values from -24 to 24
- documents: int32 [65536], P(('dp', 'seq')), parts along dimension 0, may hold values from 0 to 7, never falling along the last dimension, each value on 1 to 6144 neighbouring positions
- global_offsets: int32 [1024], P(('dp', 'seq')), parts along dimension 0, may hold values from 0 to 127
Outputs:
- attended: bfloat16 [65536, 2048], P(('dp', 'seq')), parts along dimension 0
- query_grad: bfloat16 [65536, 2048], P(('dp', 'seq')), parts along dimension 0
- key_grad: bfloat16 [65536, 2048], P(('dp', 'seq')), parts along dimension 0
- value_grad: bfloat16 [65536, 2048], P(('dp', 'seq')), parts along dimension 0
There are 8 independent parts, one for each index of `dp`. A program takes and returns all parts, laid end to end along the dimension named above; each array names one. Nothing has to cross between parts.
All inputs are finite; a program needn't handle non-finite values.
Results may differ from a plain program's by a relative error of at most 0.023.
Values may be sent and summed in bfloat16 or wider, within the bound.
No kernel may reach another device: no remote copies, remote signals or barrier semaphores. Data moves between devices by JAX's collectives and lax.ppermute only.
A program may use at most 64 MiB of HBM per device.

v0:
```python
import jax
import jax.numpy as jnp
from jax import lax
from jax.sharding import PartitionSpec as P

HEADS = 16
LEVELS = 2


def from_partner(array, axis, stride):
    return lax.ppermute(array, axis, [(i, i ^ 1 << stride) for i in range(lax.axis_size(axis))])


def local(queries, keys, values, cotangent, documents, global_offsets):
    rows_here, columns = queries.shape
    head_size = columns // HEADS
    temper = head_size ** (-0.5)
    shards = lax.axis_size("seq")
    myself = lax.axis_index("seq")
    log_shards = shards.bit_length() - 1
    level_bits = [step * (log_shards - 2) // (LEVELS - 1) for step in range(LEVELS)]

    def split(array):
        return array.reshape(array.shape[0], HEADS, head_size)

    every_doc = lax.all_gather(documents, "seq", axis=0, tiled=True)
    picked_keys = keys[global_offsets]
    picked_values = values[global_offsets]
    global_keys, global_values = (
        lax.all_gather(picked_keys, "seq", axis=0, tiled=True),
        lax.all_gather(picked_values, "seq", axis=0, tiled=True),
    )
    global_count = global_keys.shape[0]
    per_block = global_offsets.shape[0]
    owners = jnp.arange(global_count, dtype=jnp.int32) // per_block
    distance = owners ^ myself
    nearby = distance == 0
    for level_bit in level_bits:
        nearby = nearby | (distance == 1 << level_bit)
    query_heads = split(queries)
    dout_heads = split(cotangent)
    key_list = [keys]
    value_list = [values]
    mask_list = [documents[:, None] == documents[None, :]]
    for level_bit in level_bits:
        partner_keys, partner_values = from_partner((keys, values), "seq", level_bit)
        partner_docs = lax.dynamic_slice_in_dim(
            every_doc, (myself ^ 1 << level_bit) * rows_here, rows_here
        )
        key_list.append(partner_keys)
        value_list.append(partner_values)
        mask_list.append(documents[:, None] == partner_docs[None, :])
    block_keys = jnp.concatenate(key_list, 0)
    block_values = jnp.concatenate(value_list, 0)
    block_mask = jnp.concatenate(mask_list, 1)
    raw = (
        jnp.einsum(
            "thd,uhd->htu", query_heads, split(block_keys), preferred_element_type=jnp.float32
        )
        * temper
    )
    block_scores = jnp.where(block_mask[None], raw, -jnp.inf)
    global_raw = (
        jnp.einsum(
            "thd,ghd->htg", query_heads, split(global_keys), preferred_element_type=jnp.float32
        )
        * temper
    )
    global_scores = jnp.where(jnp.logical_not(nearby)[None, None, :], global_raw, -jnp.inf)
    highest = jnp.maximum(jnp.max(global_scores, axis=-1), jnp.max(block_scores, axis=-1))
    block_exp = jnp.exp(block_scores - highest[..., None])
    global_exp = jnp.exp(global_scores - highest[..., None])
    totals = jnp.sum(global_exp, axis=-1) + jnp.sum(block_exp, axis=-1)
    probs = block_exp / totals[..., None]
    global_prob = global_exp / totals[..., None]
    probs_b = probs.astype(jnp.bfloat16)
    global_prob_b = global_prob.astype(jnp.bfloat16)
    summed = jnp.einsum(
        "htg,ghd->thd", global_prob_b, split(global_values), preferred_element_type=jnp.float32
    )
    summed = summed + jnp.einsum(
        "htu,uhd->thd", probs_b, split(block_values), preferred_element_type=jnp.float32
    )
    attended = summed.astype(jnp.bfloat16).reshape(rows_here, columns)
    delta = jnp.sum(dout_heads.astype(jnp.float32) * split(attended).astype(jnp.float32), axis=-1).T
    product = jnp.einsum(
        "thd,uhd->htu", dout_heads, split(block_values), preferred_element_type=jnp.float32
    )
    slope = (probs * (product - delta[:, :, None])).astype(jnp.bfloat16)
    query_term = jnp.einsum(
        "htu,uhd->thd", slope, split(block_keys), preferred_element_type=jnp.float32
    )
    key_term = temper * jnp.einsum(
        "htu,thd->uhd", slope, query_heads, preferred_element_type=jnp.float32
    )
    value_term = jnp.einsum("htu,thd->uhd", probs_b, dout_heads, preferred_element_type=jnp.float32)
    query_sum = query_term
    key_sum = key_term[:rows_here]
    value_sum = value_term[:rows_here]
    for level, level_bit in enumerate(level_bits):
        lower = (level + 1) * rows_here
        upper = (level + 2) * rows_here
        back_keys, back_values = from_partner(
            (
                key_term[lower:upper].reshape(rows_here, columns).astype(jnp.bfloat16),
                value_term[lower:upper].reshape(rows_here, columns).astype(jnp.bfloat16),
            ),
            "seq",
            level_bit,
        )
        key_sum = key_sum + split(back_keys).astype(jnp.float32)
        value_sum = value_sum + split(back_values).astype(jnp.float32)
    global_product = jnp.einsum(
        "thd,ghd->htg", dout_heads, split(global_values), preferred_element_type=jnp.float32
    )
    global_slope = (global_prob * (global_product - delta[:, :, None])).astype(jnp.bfloat16)
    query_sum = query_sum + jnp.einsum(
        "htg,ghd->thd", global_slope, split(global_keys), preferred_element_type=jnp.float32
    )
    key_part = temper * jnp.einsum(
        "htg,thd->ghd", global_slope, query_heads, preferred_element_type=jnp.float32
    )
    value_part = jnp.einsum(
        "htg,thd->ghd", global_prob_b, dout_heads, preferred_element_type=jnp.float32
    )
    owned = lax.psum_scatter(
        jnp.concatenate(
            [
                key_part.reshape(per_block * lax.axis_size("seq"), columns),
                value_part.reshape(per_block * lax.axis_size("seq"), columns),
            ],
            1,
        ),
        "seq",
        scatter_dimension=0,
        tiled=True,
    )
    placement = (jnp.arange(rows_here, dtype=jnp.int32)[:, None] == global_offsets[None, :]).astype(
        jnp.float32
    )
    spread_rows = jnp.dot(
        placement, owned, precision=lax.Precision.HIGHEST, preferred_element_type=jnp.float32
    )
    key_grad = (key_sum.reshape(rows_here, columns) + spread_rows[:, :columns]).astype(jnp.bfloat16)
    value_grad = (value_sum.reshape(rows_here, columns) + spread_rows[:, columns:]).astype(
        jnp.bfloat16
    )
    query_grad = (temper * query_sum).reshape(rows_here, columns).astype(jnp.bfloat16)
    return (attended, query_grad, key_grad, value_grad)


def solution(mesh):
    in_specs = (
        P(("dp", "seq"), None),
        P(("dp", "seq"), None),
        P(("dp", "seq"), None),
        P(("dp", "seq"), None),
        P(("dp", "seq")),
        P(("dp", "seq")),
    )
    out_specs = (
        P(("dp", "seq"), None),
        P(("dp", "seq"), None),
        P(("dp", "seq"), None),
        P(("dp", "seq"), None),
    )
    return jax.shard_map(local, mesh=mesh, in_specs=in_specs, out_specs=out_specs, check_vma=False)
```

profile of v0, /device:TPU:1, one launch (start us, length us, event | category | flops | bytes accessed | tf_op | source)
XLA Modules:
  0.0 1265.3 jit_solution(16097213967234120717)
XLA Ops:
  7.2 1.4 copy.77
  8.6 5.7 collective-permute-start.1
  14.3 5.0 collective-permute-start
  19.3 4.5 collective-permute-start.3
  23.8 2.2 collective-permute-start.2
  26.7 1.7 gather_fusion
  28.4 1.7 gather_fusion.1
  30.1 124.5 %all-gather.2 = bf16[64,2,2048]{2,1,0:T(2,128)(2,1)S(1)} all-gather(bf16[1,2,2048]{2,1,0:T(2,128)(2,1)S(1)} %bitcast.117), channel_id=2, replica_groups=mesh['seq'=64,'dp'=8] {'seq'}, dimensions={0}, use_global_device_ids=true | all-gather | bytes 532480 | tf_op jit(solution)/shard_map/all_gather | solution.py:31
  154.6 113.8 %all-gather.3 = bf16[64,2,2048]{2,1,0:T(2,128)(2,1)S(1)} all-gather(bf16[1,2,2048]{2,1,0:T(2,128)(2,1)S(1)} %bitcast.116), channel_id=3, replica_groups=mesh['seq'=64,'dp'=8] {'seq'}, dimensions={0}, use_global_device_ids=true | all-gather | bytes 532480 | tf_op jit(solution)/shard_map/all_gather | solution.py:30
  268.4 114.1 %all-gather.4 = s32[64,1,128]{2,1,0:T(1,128)S(1)} all-gather(s32[1,1,128]{2,1,0:T(1,128)} %bitcast.118), channel_id=1, replica_groups=mesh['seq'=64,'dp'=8] {'seq'}, dimensions={0}, use_global_device_ids=true | all-gather | bytes 33280 | tf_op jit(solution)/shard_map/all_gather | solution.py:26
  382.6 0.8 broadcast_compare_fusion.2
  383.5 2.0 copy.84
  385.5 1.1 reshape.104
  387.7 1.3 dynamic-slice
  390.1 0.8 copy-done.12
  390.9 1.4 pad_maximum_fusion.1
  393.3 1.4 copy-done
  395.4 2.5 pad_maximum_fusion.2
  398.0 2.7 copy.82
  400.7 2.0 fusion.23
  403.5 2.1 multiply_reduce_fusion
  406.0 2.6 fusion
  408.6 3.2 fusion.39
  411.8 1.5 fusion.30
  413.2 2.0 copy.108
  415.3 1.5 fusion.6
  416.7 2.6 copy.103
  419.3 3.0 pad_maximum_fusion
  422.4 2.4 fusion.35
  424.8 1.9 collective-permute-start.7
  426.7 2.1 collective-permute-start.6
  428.8 2.3 fusion.40
  431.2 1.0 copy.97
  432.2 4.7 collective-permute-start.5
  437.0 1.0 copy.95
  438.0 2.2 collective-permute-start.4
  440.2 1.3 fusion.41
  441.6 2.0 fusion.12
  443.6 1.0 copy.109
  444.6 4.2 collective-permute-done.7
  448.8 1.7 fusion.16
  450.9 9.7 collective-permute-done.5
  460.8 1.2 copy.96
  462.0 2.4 fusion.18
  464.4 1.6 copy.99
  466.3 787.9 %all-reduce.3.cloned.1.call-done = f32[128,4096]{0,1:T(8,128)} async-done(((f32[128,4096]{0,1:T(8,128)}), f32[128,4096]{0,1:T(8,128)}) %all-reduce.3.cloned.1.call-update) | async-done | bytes 2097168
  1254.2 3.0 fusion.4
  1257.2 1.2 fusion.15
  (53 shorter events, 6.1 us)
Async XLA Ops:
  7.2 380.3 %copy-start.8 = (bf16[128,2048]{1,0:T(8,128)(2,1)S(1)}, bf16[128,2048]{1,0:T(8,128)(2,1)}, u32[]{:S(2)}) copy-start(bf16[128,2048]{1,0:T(8,128)(2,1)} %param.6) | copy-start | bytes 1572868
  7.2 1247.0 %all-reduce.3.cloned.1.call-start = ((), (), s32[]{:S(2)}) async-start(), calls=%async_computation | async-start | bytes 4194304
  8.6 381.5 %collective-permute-start.1 = (bf16[128,2048]{0,1:T(8,128)(2,1)S(1)}, bf16[128,2048]{0,1:T(8,128)(2,1)S(1)}, u32[]{:S(2)}, u32[]{:S(2)}) collective-permute-start(bf16[128,2048]{0,1:T(8,128)(2,1)S(1)} %copy.77), channel_id=1, source_target_pairs={{0,128},{8,136},{16,144},{24,152},{32,160},{40,168},{48,176},{56,1... | collective-permute-start | bytes 1572872 | tf_op jit(solution)/shard_map/ppermute | solution.py:11
  14.3 376.6 %collective-permute-start = (bf16[128,2048]{0,1:T(8,128)(2,1)S(1)}, bf16[128,2048]{0,1:T(8,128)(2,1)}, u32[]{:S(2)}, u32[]{:S(2)}) collective-permute-start(bf16[128,2048]{0,1:T(8,128)(2,1)S(1)} %copy.77), channel_id=1, source_target_pairs={{0,8},{8,0},{16,24},{24,16},{32,40},{40,32},{48,56},{56,48},{64,72... | collective-permute-start | bytes 1572872 | tf_op jit(solution)/shard_map/ppermute | solution.py:11
  19.3 376.2 %collective-permute-start.3 = (bf16[128,2048]{1,0:T(8,128)(2,1)}, bf16[128,2048]{1,0:T(8,128)(2,1)}, u32[]{:S(2)}, u32[]{:S(2)}) collective-permute-start(bf16[128,2048]{1,0:T(8,128)(2,1)} %param.8), channel_id=1, source_target_pairs={{0,128},{8,136},{16,144},{24,152},{32,160},{40,168},{48,176},{56,1... | collective-permute-start | bytes 1572872 | tf_op jit(solution)/shard_map/ppermute | solution.py:11
  23.8 371.6 %collective-permute-start.2 = (bf16[128,2048]{1,0:T(8,128)(2,1)}, bf16[128,2048]{1,0:T(8,128)(2,1)}, u32[]{:S(2)}, u32[]{:S(2)}) collective-permute-start(bf16[128,2048]{1,0:T(8,128)(2,1)} %param.8), channel_id=1, source_target_pairs={{0,8},{8,0},{16,24},{24,16},{32,40},{40,32},{48,56},{56,48},{64,72... | collective-permute-start | bytes 1572872 | tf_op jit(solution)/shard_map/ppermute | solution.py:11
  390.1 3.1 copy-start.3
  390.1 0.8 copy-start.12
  393.1 1.7 copy-start
  393.1 2.3 copy-start.7
  398.0 4.7 copy-start.9
  400.6 2.4 copy-start.1
  400.6 2.8 copy-start.6
  403.5 2.1 copy-start.4
  403.5 2.1 copy-start.10
  403.5 2.1 copy-start.11
  406.0 9.3 copy-start.5
  422.4 6.4 copy-start.2
  424.8 24.0 %collective-permute-start.7 = (bf16[128,2048]{0,1:T(8,128)(2,1)}, bf16[128,2048]{0,1:T(8,128)(2,1)}, u32[]{:S(2)}, u32[]{:S(2)}) collective-permute-start(bf16[128,2048]{0,1:T(8,128)(2,1)} %bitcast.29), channel_id=1, source_target_pairs={{0,128},{8,136},{16,144},{24,152},{32,160},{40,168},{48,176},{56,1... | collective-permute-start | bytes 1572872 | tf_op jit(solution)/shard_map/ppermute | solution.py:11
  426.7 22.1 %collective-permute-start.6 = (bf16[128,2048]{0,1:T(8,128)(2,1)}, bf16[128,2048]{0,1:T(8,128)(2,1)}, u32[]{:S(2)}, u32[]{:S(2)}) collective-permute-start(bf16[128,2048]{0,1:T(8,128)(2,1)} %bitcast.27), channel_id=1, source_target_pairs={{0,8},{8,0},{16,24},{24,16},{32,40},{40,32},{48,56},{56,48},{64,72... | collective-permute-start | bytes 1572872 | tf_op jit(solution)/shard_map/ppermute | solution.py:11
  432.2 28.3 %collective-permute-start.5 = (bf16[128,2048]{0,1:T(8,128)(2,1)}, bf16[128,2048]{0,1:T(8,128)(2,1)S(1)}, u32[]{:S(2)}, u32[]{:S(2)}) collective-permute-start(bf16[128,2048]{0,1:T(8,128)(2,1)} %bitcast.112), channel_id=1, source_target_pairs={{0,128},{8,136},{16,144},{24,152},{32,160},{40,168},{48,176},{56,1... | collective-permute-start | bytes 1572872 | tf_op jit(solution)/shard_map/ppermute | solution.py:11
  438.0 22.8 %collective-permute-start.4 = (bf16[128,2048]{0,1:T(8,128)(2,1)}, bf16[128,2048]{0,1:T(8,128)(2,1)}, u32[]{:S(2)}, u32[]{:S(2)}) collective-permute-start(bf16[128,2048]{0,1:T(8,128)(2,1)} %bitcast.113), channel_id=1, source_target_pairs={{0,8},{8,0},{16,24},{24,16},{32,40},{40,32},{48,56},{56,48},{64,72... | collective-permute-start | bytes 1572872 | tf_op jit(solution)/shard_map/ppermute | solution.py:11
  464.4 789.8 %copy-start.13 = (s32[2]{0:T(128)S(1)}, s32[2]{0:T(128)}, u32[]{:S(2)}) copy-start(s32[2]{0:T(128)} %param.11) | copy-start | bytes 28
Sparse Core Ops, SparseCore 0:
  422.5 831.6 all-reduce.2
where the time goes:
time: 1270 us
  waiting for transfers between devices  802 us (63%)
  blocking collectives  352 us (28%)
  local copies, waits for them, and re-layouts  30 us (2%)
  starting transfers between devices  28.4 us (2%)
  matrix products  23 us (2%)
  between operations  15.1 us (1%)
  other arithmetic  14.6 us (1%)
    unnamed x2, waiting for transfers between devices  788 us
    all_gather x1, blocking collectives, local(): lax.all_gather(picked_values, 'seq', axis=0, tiled=True)  125 us
    all_gather x1, blocking collectives, local(): every_doc = lax.all_gather(documents, 'seq', axis=0, tiled=True)  114 us
    all_gather x1, blocking collectives, local(): lax.all_gather(picked_keys, 'seq', axis=0, tiled=True)  114 us
    ppermute x8, starting transfers between devices, from_partner(): lax.ppermute(array, axis, [(i, i ^ 1 << stride) for i in range(lax.axis_s...  28.4 us
  transfers between devices with their start and end apart: 9, of which 3 were waited for; matrix products, arithmetic and copies ran while one was open for 3% of the time, Pallas kernels for 0%

commit v1 on v0

--- a/solution.py
+++ b/solution.py
@@ -5,6 +5,11 @@
 
 HEADS = 16
 LEVELS = 2
+
+
+def swapped_in(block, name, d):
+    sent = jnp.stack([block] * lax.axis_size(name))
+    return jnp.concatenate(lax.all_to_all(sent, name, 0, 0), axis=d)
 
 
 def from_partner(array, axis, stride):
@@ -28,7 +33,7 @@
     picked_values = values[global_offsets]
     global_keys, global_values = (
         lax.all_gather(picked_keys, "seq", axis=0, tiled=True),
-        lax.all_gather(picked_values, "seq", axis=0, tiled=True),
+        swapped_in(picked_values, "seq", 0),
     )
     global_count = global_keys.shape[0]
     per_block = global_offsets.shape[0]

time: 1270 us -> 1180 us (0.929)
  blocking collectives: 352 us -> 237 us
    all_gather x1 -> x0, blocking collectives: 125 us -> none  [local(): lax.all_gather(picked_values, 'seq', axis=0, tiled=True)]
    unnamed x2, waiting for transfers between devices: 788 us -> 802 us
  transfers between devices with their start and end apart: 9 -> 10, of which waited for: 3 -> 3; matrix products, arithmetic and copies ran while one was open for 3% -> 4% of each run, Pallas kernels for 0% -> 0%
where the time goes in v1:
time: 1180 us
  waiting for transfers between devices  812 us (69%)
  blocking collectives  237 us (20%)
  starting transfers between devices  37.2 us (3%)
  local copies, waits for them, and re-layouts  32.9 us (3%)
  matrix products  27.8 us (2%)
  other arithmetic  15.1 us (1%)
  between operations  15.1 us (1%)
    unnamed x2, waiting for transfers between devices  802 us
    all_gather x1, blocking collectives, local(): lax.all_gather(picked_keys, 'seq', axis=0, tiled=True)  125 us
    all_gather x1, blocking collectives, local(): every_doc = lax.all_gather(documents, 'seq', axis=0, tiled=True)  112 us
    ppermute x8, starting transfers between devices, from_partner(): lax.ppermute(array, axis, [(i, i ^ 1 << stride) for i in range(lax.axis_s...  26.7 us
  transfers between devices with their start and end apart: 10, of which 3 were waited for; matrix products, arithmetic and copies ran while one was open for 4% of the time, Pallas kernels for 0%

profile of v1, /device:TPU:1, one launch (start us, length us, event | category | flops | bytes accessed | tf_op | source)
XLA Modules:
  0.0 1177.3 jit_solution(1356985948944871817)
XLA Ops:
  7.2 1.4 copy.77
  8.6 5.7 collective-permute-start.1
  14.3 5.0 collective-permute-start
  19.3 4.5 collective-permute-start.3
  23.8 2.2 collective-permute-start.2
  26.7 1.7 gather_fusion
  28.4 1.1 stack.2
  29.5 10.4 all-to-all-start
  39.9 1.7 gather_fusion.1
  41.6 124.8 %all-gather.1 = bf16[64,2,2048]{2,1,0:T(2,128)(2,1)S(1)} all-gather(bf16[1,2,2048]{2,1,0:T(2,128)(2,1)S(1)} %bitcast.115), channel_id=2, replica_groups=mesh['seq'=64,'dp'=8] {'seq'}, dimensions={0}, use_global_device_ids=true | all-gather | bytes 532480 | tf_op jit(solution)/shard_map/all_gather | solution.py:35
  166.4 112.5 %all-gather.2 = s32[64,1,128]{2,1,0:T(1,128)S(1)} all-gather(s32[1,1,128]{2,1,0:T(1,128)S(1)} %bitcast.116), channel_id=1, replica_groups=mesh['seq'=64,'dp'=8] {'seq'}, dimensions={0}, use_global_device_ids=true | all-gather | bytes 33280 | tf_op jit(solution)/shard_map/all_gather | solution.py:31
  281.2 1.3 dynamic-slice
  284.4 1.6 pad_maximum_fusion.1
  288.2 2.8 fusion.39
  291.0 1.3 fusion.35
  292.2 1.9 collective-permute-start.7
  294.2 2.3 collective-permute-start.6
  296.5 2.5 pad_maximum_fusion.2
  299.0 2.6 copy.82
  301.6 2.8 fusion.30
  304.5 4.2 collective-permute-done.7
  308.7 2.7 fusion.16
  311.3 2.5 copy.124
  313.8 1.1 reshape_reshape.4
  315.0 2.0 fusion.23
  317.4 3.5 multiply_reduce_fusion
  320.9 2.0 copy.108
  322.9 1.8 fusion.13
  325.5 1.5 fusion.6
  327.0 2.6 copy.103
  329.6 3.0 pad_maximum_fusion
  332.6 3.7 fusion
  336.3 2.2 fusion.40
  338.7 1.0 copy.97
  339.7 2.2 collective-permute-start.5
  341.9 1.0 copy.95
  342.9 2.9 collective-permute-start.4
  345.8 1.3 fusion.41
  347.2 2.0 fusion.12
  349.2 1.0 copy.109
  350.2 5.3 collective-permute-done.5
  355.8 1.2 copy.96
  357.0 2.4 fusion.18
  359.5 2.6 copy.99
  362.1 1.6 copy.105
  363.7 802.5 %all-reduce.3.cloned.1.call-done = f32[128,4096]{0,1:T(8,128)} async-done(((f32[128,4096]{0,1:T(8,128)}), f32[128,4096]{0,1:T(8,128)}) %all-reduce.3.cloned.1.call-update) | async-done | bytes 2097168
  1166.2 3.0 fusion.4
  1169.3 1.2 fusion.15
  (57 shorter events, 8.0 us)
Async XLA Ops:
  7.2 159.3 %copy-start.13 = (s32[128]{0:T(128)S(1)}, s32[128]{0:T(128)}, u32[]{:S(2)}) copy-start(s32[128]{0:T(128)} %param.10) | copy-start | bytes 1540
  7.2 271.9 %copy-start.8 = (bf16[128,2048]{1,0:T(8,128)(2,1)S(1)}, bf16[128,2048]{1,0:T(8,128)(2,1)}, u32[]{:S(2)}) copy-start(bf16[128,2048]{1,0:T(8,128)(2,1)} %param.9) | copy-start | bytes 1572868
  7.2 273.7 %copy-start.9 = (bf16[128,2048]{1,0:T(8,128)(2,1)S(1)}, bf16[128,2048]{1,0:T(8,128)(2,1)}, u32[]{:S(2)}) copy-start(bf16[128,2048]{1,0:T(8,128)(2,1)} %param.6) | copy-start | bytes 1572868
  8.6 272.6 %copy-start.5 = (bf16[128,2048]{0,1:T(8,128)(2,1)}, bf16[128,2048]{0,1:T(8,128)(2,1)S(1)}, u32[]{:S(2)}) copy-start(bf16[128,2048]{0,1:T(8,128)(2,1)S(1)} %copy.77) | copy-start | bytes 1572868
  8.6 274.9 %collective-permute-start.1 = (bf16[128,2048]{0,1:T(8,128)(2,1)S(1)}, bf16[128,2048]{0,1:T(8,128)(2,1)S(1)}, u32[]{:S(2)}, u32[]{:S(2)}) collective-permute-start(bf16[128,2048]{0,1:T(8,128)(2,1)S(1)} %copy.77), channel_id=1, source_target_pairs={{0,128},{8,136},{16,144},{24,152},{32,160},{40,168},{48,176},{56,1... | collective-permute-start | bytes 1572872 | tf_op jit(solution)/shard_map/ppermute | solution.py:16
  14.3 270.1 %collective-permute-start = (bf16[128,2048]{0,1:T(8,128)(2,1)S(1)}, bf16[128,2048]{0,1:T(8,128)(2,1)}, u32[]{:S(2)}, u32[]{:S(2)}) collective-permute-start(bf16[128,2048]{0,1:T(8,128)(2,1)S(1)} %copy.77), channel_id=1, source_target_pairs={{0,8},{8,0},{16,24},{24,16},{32,40},{40,32},{48,56},{56,48},{64,72... | collective-permute-start | bytes 1572872 | tf_op jit(solution)/shard_map/ppermute | solution.py:16
  19.3 277.1 %collective-permute-start.3 = (bf16[128,2048]{1,0:T(8,128)(2,1)}, bf16[128,2048]{1,0:T(8,128)(2,1)}, u32[]{:S(2)}, u32[]{:S(2)}) collective-permute-start(bf16[128,2048]{1,0:T(8,128)(2,1)} %param.8), channel_id=1, source_target_pairs={{0,128},{8,136},{16,144},{24,152},{32,160},{40,168},{48,176},{56,1... | collective-permute-start | bytes 1572872 | tf_op jit(solution)/shard_map/ppermute | solution.py:16
  23.8 272.6 %collective-permute-start.2 = (bf16[128,2048]{1,0:T(8,128)(2,1)}, bf16[128,2048]{1,0:T(8,128)(2,1)}, u32[]{:S(2)}, u32[]{:S(2)}) collective-permute-start(bf16[128,2048]{1,0:T(8,128)(2,1)} %param.8), channel_id=1, source_target_pairs={{0,8},{8,0},{16,24},{24,16},{32,40},{40,32},{48,56},{56,48},{64,72... | collective-permute-start | bytes 1572872 | tf_op jit(solution)/shard_map/ppermute | solution.py:16
  29.5 284.4 %all-to-all-start = ((bf16[64,2,2048]{2,1,0:T(2,128)(2,1)}), bf16[64,2,2048]{2,1,0:T(2,128)(2,1)S(1)}, u32[]{:S(2)}, u32[]{:S(2)}) async-start(bf16[64,2,2048]{2,1,0:T(2,128)(2,1)} %stack.2), calls=%async_computation | async-start | bytes 1048576 | tf_op jit(solution)/shard_map/all_to_all | solution.py:12
  39.9 1126.3 %all-reduce.3.cloned.1.call-start = ((), (), s32[]{:S(2)}) async-start(), calls=%async_computation.1 | async-start | bytes 4194304
  283.5 3.3 copy-start.4
  283.6 0.8 copy-start.12
  286.8 4.2 copy-start
  286.8 1.4 copy-start.10
  288.2 8.2 copy-start.7
  292.2 16.4 %collective-permute-start.7 = (bf16[128,2048]{0,1:T(8,128)(2,1)}, bf16[128,2048]{0,1:T(8,128)(2,1)}, u32[]{:S(2)}, u32[]{:S(2)}) collective-permute-start(bf16[128,2048]{0,1:T(8,128)(2,1)} %bitcast.28), channel_id=1, source_target_pairs={{0,128},{8,136},{16,144},{24,152},{32,160},{40,168},{48,176},{56,1... | collective-permute-start | bytes 1572872 | tf_op jit(solution)/shard_map/ppermute | solution.py:16
  294.2 14.5 %collective-permute-start.6 = (bf16[128,2048]{0,1:T(8,128)(2,1)}, bf16[128,2048]{0,1:T(8,128)(2,1)}, u32[]{:S(2)}, u32[]{:S(2)}) collective-permute-start(bf16[128,2048]{0,1:T(8,128)(2,1)} %bitcast.26), channel_id=1, source_target_pairs={{0,8},{8,0},{16,24},{24,16},{32,40},{40,32},{48,56},{56,48},{64,72... | collective-permute-start | bytes 1572872 | tf_op jit(solution)/shard_map/ppermute | solution.py:16
  315.0 2.4 copy-start.1
  315.0 2.5 copy-start.11
  324.7 0.8 copy-start.6
  336.3 2.3 copy-start.2
  339.7 15.9 %collective-permute-start.5 = (bf16[128,2048]{0,1:T(8,128)(2,1)}, bf16[128,2048]{0,1:T(8,128)(2,1)S(1)}, u32[]{:S(2)}, u32[]{:S(2)}) collective-permute-start(bf16[128,2048]{0,1:T(8,128)(2,1)} %bitcast.111), channel_id=1, source_target_pairs={{0,128},{8,136},{16,144},{24,152},{32,160},{40,168},{48,176},{56,1... | collective-permute-start | bytes 1572872 | tf_op jit(solution)/shard_map/ppermute | solution.py:16
  342.9 12.9 %collective-permute-start.4 = (bf16[128,2048]{0,1:T(8,128)(2,1)}, bf16[128,2048]{0,1:T(8,128)(2,1)}, u32[]{:S(2)}, u32[]{:S(2)}) collective-permute-start(bf16[128,2048]{0,1:T(8,128)(2,1)} %bitcast.112), channel_id=1, source_target_pairs={{0,8},{8,0},{16,24},{24,16},{32,40},{40,32},{48,56},{56,48},{64,72... | collective-permute-start | bytes 1572872 | tf_op jit(solution)/shard_map/ppermute | solution.py:16
  359.5 806.7 %copy-start.14 = (s32[2]{0:T(128)S(1)}, s32[2]{0:T(128)}, u32[]{:S(2)}) copy-start(s32[2]{0:T(128)} %param.11) | copy-start | bytes 28
  362.1 807.2 %copy-start.3 = (f32[128,2048]{1,0:T(8,128)S(1)}, f32[128,2048]{1,0:T(8,128)}, u32[]{:S(2)}) copy-start(f32[128,2048]{1,0:T(8,128)} %copy.124) | copy-start | bytes 3145732
Sparse Core Ops, SparseCore 0:
  332.7 833.4 all-reduce.2
